TPU v7x, 512 devices: a whole 4x8x8 slice. The times are simulated.
512 devices in a mesh: dp: 16 (over z, core), expert: 32 (over x, y).
Axes of the slice: x: 4, y: 8, z: 8, core: 2. Of those that a mesh axis runs over, the one named last changes fastest.
Arguments:
- residual_in: bfloat16 [16384, 2048], P(('dp', 'expert')), may hold values from -6 to 6
- attention_out: bfloat16 [16384, 2048], P(('dp', 'expert')), may hold values from -6 to 6
- out_weight: bfloat16 [2048, 2048], P(None, 'dp'), may hold values from -0.125 to 0.125
- post_gain: float32 [2048], replicated, may hold values from 0.1 to 1.9
- router_weight: bfloat16 [2048, 32], replicated, may hold values from -0.125 to 0.125
- expert_ids: int32 [16384, 6], P(('dp', 'expert')), may hold values from 0 to 31, all different within a row; in each aligned block of 32 rows (0 to 31, 32 to 63, ...) at most 12 rows name the same one
- expert_slot: int32 [32], replicated, may hold values from 0 to 31, each once
- expert_gate_up: bfloat16 [32, 2048, 1408], P('expert', 'dp'), may hold values from -0.125 to 0.125
- expert_down: bfloat16 [32, 704, 2048], P('expert', None, 'dp'), may hold values from -0.21875 to 0.21875
- shared_gate_up: bfloat16 [2048, 2, 2816], P(None, None, 'dp'), may hold values from -0.125 to 0.125
- shared_down: bfloat16 [2816, 2048], P(None, 'dp'), may hold values from -0.109375 to 0.109375
- final_gain: float32 [2048], replicated, may hold values from 0.1 to 1.9
Outputs:
- mixed: bfloat16 [16384, 2048], P(('dp', 'expert'))
Inputs may be any that keep to these rules, and one draw needn't show every extreme that they name: `expert_ids`: each row names 6 different experts. In each aligned block of 32 rows (the rows of one device) no expert is named by more than 12 rows, a bound that some block reaches. A permutation: expert e is held in slot expert_slot[e].
All inputs are finite; a program needn't handle non-finite values.
Results may differ from a plain program's by a relative error of at most 0.0069.
Values may be sent and summed in bfloat16 or wider, within the bound.
No kernel may reach another device: no remote copies, remote signals or barrier semaphores. Data moves between devices by JAX's collectives and lax.ppermute only.
A program may use at most 64 MiB of HBM per device.

v0:
```python
import jax
import jax.numpy as jnp
from jax import lax
from jax.sharding import PartitionSpec as P

EPS = 1e-06


def core_groups(axis):
    n = lax.axis_size(axis)
    return [list(range(0, n, 2)), list(range(1, n, 2))]


def with_sibling(blocks, axis):
    other = lax.ppermute(blocks, axis, [(i, i ^ 1) for i in range(lax.axis_size(axis))])
    pair = jnp.stack([blocks, other], axis=1)
    pair = jnp.where(lax.axis_index(axis) % 2 == 0, pair, jnp.flip(pair, axis=1))
    return pair.reshape(-1, *blocks.shape[1:])


def pair_gather(array, axis):
    blocks = lax.all_gather(array, axis, axis=0, axis_index_groups=core_groups(axis))
    return with_sibling(blocks, axis)


def pair_collect(array, axis):
    copies = jnp.broadcast_to(array, (lax.axis_size(axis) // 2, *array.shape))
    blocks = lax.all_to_all(copies, axis, 0, 0, tiled=True, axis_index_groups=core_groups(axis))
    return with_sibling(blocks, axis)


def in_order(blocks, dim):
    shape = list(blocks.shape[1:])
    shape[dim] *= blocks.shape[0]
    return jnp.moveaxis(blocks, 0, dim).reshape(shape)


def sent_to_all(array, axis):
    copies = jnp.broadcast_to(array, (lax.axis_size(axis), *array.shape))
    return lax.all_to_all(copies, axis, split_axis=0, concat_axis=0, tiled=True)


def collect(array, axis, dim):
    return in_order(sent_to_all(array, axis), dim)


def turned_gather(arrays, axis, dims):
    turned = [jnp.moveaxis(a, dim, 0) for a, dim in zip(arrays, dims)]
    widths = [t[0].size for t in turned]
    both = jnp.concatenate([t.reshape(-1, w) for t, w in zip(turned, widths)], axis=1)
    out = lax.all_gather(both, axis, axis=0, tiled=True)
    blocks = jnp.split(out, [sum(widths[:k]) for k in range(1, len(widths))], axis=1)
    return tuple(
        (
            jnp.moveaxis(b.reshape(-1, *t.shape[1:]), 0, dim)
            for b, t, dim in zip(blocks, turned, dims)
        )
    )


def rms_scale(values, gain):
    values = values.astype(jnp.float32)
    inverse = lax.rsqrt(jnp.mean(values * values, axis=-1, keepdims=True) + EPS)
    return values * inverse * gain


def per_device(
    residual_in,
    attention_out,
    out_weight,
    post_gain,
    router_weight,
    expert_ids,
    expert_slot,
    expert_gate_up,
    expert_down,
    shared_gate_up,
    shared_down,
    final_gain,
):
    rows = residual_in.shape[0]
    width = residual_in.shape[1]
    experts = router_weight.shape[1]
    choose = expert_ids.shape[1]
    capacity = max(2, min(rows, 2 * rows * choose // experts))
    proj_cols = jnp.dot(
        in_order(pair_collect(attention_out, "dp"), 0),
        out_weight,
        preferred_element_type=jnp.float32,
    ).astype(jnp.bfloat16)
    proj = lax.all_to_all(proj_cols, "dp", split_axis=0, concat_axis=1, tiled=True)
    resid = (residual_in.astype(jnp.float32) + proj.astype(jnp.float32)).astype(jnp.bfloat16)
    normed = rms_scale(resid, post_gain).astype(jnp.bfloat16)
    logits = jnp.dot(normed, router_weight, preferred_element_type=jnp.float32)
    expert_range = jnp.arange(experts, dtype=jnp.int32)
    ids = expert_ids + (proj_cols[0, 0] * 0).astype(expert_ids.dtype)
    picked = ids[:, :, None] == expert_range[None, None, :]
    chosen = jnp.sum(jnp.where(picked, logits[:, None, :], 0.0), axis=2)
    raised = jnp.exp(chosen)
    gates = raised / jnp.sum(raised, axis=1, keepdims=True)
    slots = jnp.sum(jnp.where(picked, expert_slot[None, None, :], 0), axis=2).reshape(-1)
    marked = (slots[:, None] == expert_range[None, :]).astype(jnp.int32)
    before = jnp.cumsum(marked, axis=0) - marked
    position = jnp.sum(before * marked, axis=1)
    target = slots * capacity + position
    placed = target[:, None] == jnp.arange(experts * capacity, dtype=jnp.int32)[None, :]
    select = jnp.any(placed.reshape(rows, choose, experts * capacity), axis=1).astype(jnp.bfloat16)
    outgoing = jnp.einsum("rs,rd->sd", select, normed, preferred_element_type=jnp.float32)
    outgoing = outgoing.astype(jnp.bfloat16).reshape(experts, capacity, width)
    hidden_units = expert_down.shape[1]
    weights_part = jnp.concatenate([expert_gate_up[0], expert_down[0].T], axis=1)
    weights_full = lax.all_gather(weights_part, "dp", axis=0, tiled=True)
    gate_up_full = weights_full[:, : 2 * hidden_units]
    down_turned_full = weights_full[:, 2 * hidden_units :]
    received = lax.all_to_all(outgoing, "expert", split_axis=0, concat_axis=0, tiled=True)
    sources, count, _ = received.shape
    flat = received.reshape(sources * count, width)
    both = jnp.dot(flat, gate_up_full, preferred_element_type=jnp.float32)
    active = (jax.nn.silu(both[:, :hidden_units]) * both[:, hidden_units:]).astype(jnp.bfloat16)
    result = lax.dot_general(
        active, down_turned_full, (((1,), (1,)), ((), ())), preferred_element_type=jnp.float32
    ).astype(jnp.bfloat16)
    result = result.reshape(sources, count, width)
    returned = lax.all_to_all(result, "expert", split_axis=0, concat_axis=0, tiled=True)
    shared_units = shared_gate_up.shape[2]
    shared_pair = shared_gate_up.reshape(width, 2 * shared_units)
    normed_shared = normed + (weights_full[0, 0] * 0 + outgoing[0, 0, 0] * 0).astype(normed.dtype)
    both = jnp.dot(
        in_order(pair_gather(normed_shared, "dp"), 0),
        shared_pair,
        preferred_element_type=jnp.float32,
    )
    shared_hidden = (jax.nn.silu(both[:, :shared_units]) * both[:, shared_units:]).astype(
        jnp.bfloat16
    )
    out_cols = jnp.dot(
        in_order(pair_gather(shared_hidden, "dp"), 1),
        shared_down,
        preferred_element_type=jnp.float32,
    )
    shared_out = lax.all_to_all(
        out_cols.astype(jnp.bfloat16), "dp", split_axis=0, concat_axis=1, tiled=True
    ).astype(jnp.float32)
    weighted = jnp.sum(placed.reshape(rows, choose, experts * capacity) * gates[:, :, None], axis=1)
    routed = jnp.dot(
        weighted,
        returned.reshape(experts * capacity, width).astype(jnp.float32),
        precision=lax.Precision.HIGHEST,
        preferred_element_type=jnp.float32,
    )
    total = resid.astype(jnp.float32) + routed + shared_out
    return rms_scale(total, final_gain).astype(jnp.bfloat16)


def solution(mesh):
    in_specs = (
        P(("dp", "expert"), None),
        P(("dp", "expert"), None),
        P(None, "dp"),
        P(),
        P(),
        P(("dp", "expert"), None),
        P(),
        P("expert", "dp", None),
        P("expert", None, "dp"),
        P(None, None, "dp"),
        P(None, "dp"),
        P(),
    )
    out_specs = P(("dp", "expert"), None)
    return jax.shard_map(
        per_device, mesh=mesh, in_specs=in_specs, out_specs=out_specs, check_vma=False
    )
```

profile of v0, /device:TPU:1, one launch (start us, length us, event | category | flops | bytes accessed | tf_op | source)
XLA Modules:
  0.0 248.7 jit_solution(5507769714941726172)
XLA Ops:
  6.5 1.2 copy.43
  7.7 1.8 pad_maximum_fusion.3
  9.7 44.2 %all_to_all.41 = bf16[8,32,2048]{2,1,0:T(8,128)(2,1)S(1)} all-to-all(bf16[8,32,2048]{2,1,0:T(8,128)(2,1)S(1)} %broadcast_in_dim.26), channel_id=1, replica_groups={{0,64,128,192,256,320,384,448},{32,96,160,224,288,352,416,480},{1,65,12..., dimensions={0} | all-to-all | bytes 2097152 | tf_op jit(solution)/shard_map/all_to_all | solution.py:28
  53.9 5.5 %collective-permute-start = (bf16[8,32,2048]{2,1,0:T(8,128)(2,1)S(1)}, bf16[8,32,2048]{2,1,0:T(8,128)(2,1)S(1)}, u32[]{:S(2)}, u32[]{:S(2)}) collective-permute-start(bf16[8,32,2048]{2,1,0:T(8,128)(2,1)S(1)} %all_to_all.41), channel_id=1, source_target_pairs={{0,32},{32,0},{64,96},{96,64},{128,160},{160,128},{192,224},{224,1... | collective-permute-start | bytes 3145736 | tf_op jit(solution)/shard_map/ppermute | solution.py:15
  59.5 2.3 collective-permute-done
  63.0 1.4 convolution_convert_fusion.1
  64.4 1.2 slice.48
  66.1 3.7 %all-to-all-start.1 = ((bf16[16,32,128]{2,1,0:T(8,128)(2,1)}), bf16[16,32,128]{2,1,0:T(8,128)(2,1)S(1)}, u32[]{:S(2)}, u32[]{:S(2)}) async-start(bf16[16,32,128]{2,1,0:T(8,128)(2,1)} %bitcast.4), calls=%async_computation.1 | async-start | bytes 262144 | tf_op jit(solution)/shard_map/all_to_all | solution.py:91
  71.6 8.8 %all-to-all-done.1 = bf16[16,32,128]{2,1,0:T(8,128)(2,1)S(1)} async-done(((bf16[16,32,128]{2,1,0:T(8,128)(2,1)}), bf16[16,32,128]{2,1,0:T(8,128)(2,1)S(1)}, u32[]{:S(2)}, u32[]{:S(2)}) %all-to-all-start.1) | async-done | bytes 131104 | tf_op jit(solution)/shard_map/all_to_all | solution.py:91
  81.3 1.6 reshape.112
  84.7 8.7 %all-gather.6.cloned.1.call-done = bf16[2048,2112]{1,0:T(8,128)(2,1)} async-done(((bf16[128,2112]{1,0:T(8,128)(2,1)}), bf16[2048,2112]{1,0:T(8,128)(2,1)}) %all-gather.6.cloned.1.call-update) | async-done | bytes 8650768 | tf_op jit(solution)/shard_map/all_gather | solution.py:112
  93.4 1.2 slice.55
  96.1 9.7 %all-to-all-start.2 = ((bf16[32,12,2048]{2,1,0:T(8,128)(2,1)}), bf16[32,12,2048]{2,1,0:T(8,128)(2,1)S(1)}, u32[]{:S(2)}, u32[]{:S(2)}) async-start(bf16[32,12,2048]{2,1,0:T(8,128)(2,1)} %reshape.112), calls=%async_computation.2 | async-start | bytes 4194304 | tf_op jit(solution)/shard_map/all_to_all | solution.py:115
  105.8 26.9 %all-gather.8.cloned.1.call-done = bf16[256,2048]{1,0:T(8,128)(2,1)} async-done(((bf16[32,2048]{1,0:T(8,128)(2,1)}), bf16[256,2048]{1,0:T(8,128)(2,1)}) %all-gather.8.cloned.1.call-update) | async-done | bytes 1048592 | tf_op jit(solution)/shard_map/all_gather | solution.py:22
  132.8 6.4 %collective-permute-start.1 = (bf16[8,32,2048]{2,1,0:T(8,128)(2,1)}, bf16[8,32,2048]{2,1,0:T(8,128)(2,1)S(1)}, u32[]{:S(2)}, u32[]{:S(2)}) collective-permute-start(bf16[8,32,2048]{2,1,0:T(8,128)(2,1)} %bitcast.86), channel_id=1, source_target_pairs={{0,32},{32,0},{64,96},{96,64},{128,160},{160,128},{192,224},{224,1... | collective-permute-start | bytes 3145736 | tf_op jit(solution)/shard_map/ppermute | solution.py:15
  139.2 2.5 collective-permute-done.1
  141.6 1.4 pad_maximum_fusion.2
  145.4 9.3 %all-to-all-done.2 = bf16[32,12,2048]{2,1,0:T(8,128)(2,1)S(1)} async-done(((bf16[32,12,2048]{2,1,0:T(8,128)(2,1)}), bf16[32,12,2048]{2,1,0:T(8,128)(2,1)S(1)}, u32[]{:S(2)}, u32[]{:S(2)}) %all-to-all-start.2) | async-done | bytes 1572896 | tf_op jit(solution)/shard_map/all_to_all | solution.py:115
  154.7 1.3 reshape.113
  156.0 5.8 %fusion = f32[384,1408]{1,0:T(8,128)S(1)} fusion(bf16[384,2048]{1,0:T(8,128)(2,1)} %reshape.113, bf16[2048,2112]{1,0:T(8,128)(2,1)} %all-gather.6.cloned.1.call-done), kind=kOutput, calls=%fused_computation | convolution fusion | flops 2214592512 | bytes 9502720 | tf_op jit(solution)/shard_map/dot_general | solution.py:118
  161.8 3.3 %fusion.4 = bf16[384,2048]{1,0:T(8,128)(2,1)S(1)} fusion(bf16[2048,2112]{1,0:T(8,128)(2,1)} %all-gather.6.cloned.1.call-done, f32[384,1408]{1,0:T(8,128)S(1)} %fusion), kind=kOutput, calls=%fused_computation.8 | convolution fusion | flops 1109704704 | bytes 7077888 | tf_op jit(solution)/shard_map/dot_general | solution.py:120
  165.2 1.5 reshape.114
  166.7 7.5 %all-to-all-start.3 = ((bf16[32,12,2048]{2,1,0:T(8,128)(2,1)}), bf16[32,12,2048]{2,1,0:T(8,128)(2,1)S(1)}, u32[]{:S(2)}, u32[]{:S(2)}) async-start(bf16[32,12,2048]{2,1,0:T(8,128)(2,1)} %reshape.114), calls=%async_computation.3 | async-start | bytes 4194304 | tf_op jit(solution)/shard_map/all_to_all | solution.py:124
  174.2 7.8 %all-gather.10.cloned.1.call-done = bf16[4096,176]{0,1:T(8,128)(2,1)} async-done(((bf16[512,176]{0,1:T(8,128)(2,1)}), bf16[4096,176]{0,1:T(8,128)(2,1)}) %all-gather.10.cloned.1.call-update) | async-done | bytes 1441808 | tf_op jit(solution)/shard_map/all_gather | solution.py:22
  182.0 1.6 copy.60
  183.6 7.3 %collective-permute-start.2 = (bf16[8,512,176]{1,2,0:T(8,128)(2,1)S(1)}, bf16[8,512,176]{1,2,0:T(8,128)(2,1)S(1)}, u32[]{:S(2)}, u32[]{:S(2)}) collective-permute-start(bf16[8,512,176]{1,2,0:T(8,128)(2,1)S(1)} %bitcast.83), channel_id=1, source_target_pairs={{0,32},{32,0},{64,96},{96,64},{128,160},{160,128},{192,224},{224,1... | collective-permute-start | bytes 4325384 | tf_op jit(solution)/shard_map/ppermute | solution.py:15
  195.0 1.6 convolution_convert_fusion.2
  196.6 26.5 %all-to-all-done.3 = bf16[32,12,2048]{2,1,0:T(8,128)(2,1)S(1)} async-done(((bf16[32,12,2048]{2,1,0:T(8,128)(2,1)}), bf16[32,12,2048]{2,1,0:T(8,128)(2,1)S(1)}, u32[]{:S(2)}, u32[]{:S(2)}) %all-to-all-start.3) | async-done | bytes 1572896 | tf_op jit(solution)/shard_map/all_to_all | solution.py:124
  223.1 6.7 %all-to-all-start.4 = ((bf16[16,32,128]{2,1,0:T(8,128)(2,1)}), bf16[16,32,128]{2,1,0:T(8,128)(2,1)}, u32[]{:S(2)}, u32[]{:S(2)}) async-start(bf16[16,32,128]{2,1,0:T(8,128)(2,1)} %bitcast.90), calls=%async_computation.4 | async-start | bytes 262144 | tf_op jit(solution)/shard_map/all_to_all | solution.py:141
  230.5 1.3 reshape.115
  231.8 7.2 %all-to-all-done.4 = bf16[16,32,128]{2,1,0:T(8,128)(2,1)} async-done(((bf16[16,32,128]{2,1,0:T(8,128)(2,1)}), bf16[16,32,128]{2,1,0:T(8,128)(2,1)}, u32[]{:S(2)}, u32[]{:S(2)}) %all-to-all-start.4) | async-done | bytes 131104 | tf_op jit(solution)/shard_map/all_to_all | solution.py:141
  239.0 2.4 multiply_reduce_fusion
  (75 shorter events, 13.7 us)
Async XLA Ops:
  6.5 137.1 %copy-start = (bf16[2048,2,176]{0,2,1:T(8,128)(2,1)S(1)}, bf16[2048,2,176]{0,2,1:T(8,128)(2,1)}, u32[]{:S(2)}) copy-start(bf16[2048,2,176]{0,2,1:T(8,128)(2,1)} %param.21) | copy-start | bytes 4325380
  6.5 3.0 %copy-start.6 = (bf16[32,2048]{1,0:T(8,128)(2,1)S(1)}, bf16[32,2048]{1,0:T(8,128)(2,1)}, u32[]{:S(2)}) copy-start(bf16[32,2048]{1,0:T(8,128)(2,1)} %param.13) | copy-start | bytes 393220
  6.5 86.9 %all-gather.6.cloned.1.call-start = ((), (), s32[]{:S(2)}) async-start(), calls=%async_computation.5 | async-start | bytes 9469952 | tf_op jit(solution)/shard_map/all_gather | solution.py:112
  53.9 7.8 %collective-permute-start = (bf16[8,32,2048]{2,1,0:T(8,128)(2,1)S(1)}, bf16[8,32,2048]{2,1,0:T(8,128)(2,1)S(1)}, u32[]{:S(2)}, u32[]{:S(2)}) collective-permute-start(bf16[8,32,2048]{2,1,0:T(8,128)(2,1)S(1)} %all_to_all.41), channel_id=1, source_target_pairs={{0,32},{32,0},{64,96},{96,64},{128,160},{160,128},{192,224},{224,1... | collective-permute-start | bytes 3145736 | tf_op jit(solution)/shard_map/ppermute | solution.py:15
  62.0 1.0 copy-start.5
  62.5 7.3 %copy-start.10 = (s32[32,6]{0,1:T(8,128)S(1)}, s32[32,6]{0,1:T(8,128)}, u32[]{:S(2)}) copy-start(s32[32,6]{0,1:T(8,128)} %param.17) | copy-start | bytes 2308
  62.6 7.3 %copy-start.13 = (s32[32]{0:T(128)S(1)}, s32[32]{0:T(128)}, u32[]{:S(2)}) copy-start(s32[32]{0:T(128)} %param.18) | copy-start | bytes 388
  62.6 17.9 %copy-start.7 = (bf16[32,2048]{1,0:T(8,128)(2,1)S(1)}, bf16[32,2048]{1,0:T(8,128)(2,1)}, u32[]{:S(2)}) copy-start(bf16[32,2048]{1,0:T(8,128)(2,1)} %param.12) | copy-start | bytes 393220
  62.6 18.1 %copy-start.8 = (f32[2048]{0:T(1024)S(1)}, f32[2048]{0:T(1024)}, u32[]{:S(2)}) copy-start(f32[2048]{0:T(1024)} %param.15) | copy-start | bytes 24580
  66.1 14.4 %all-to-all-start.1 = ((bf16[16,32,128]{2,1,0:T(8,128)(2,1)}), bf16[16,32,128]{2,1,0:T(8,128)(2,1)S(1)}, u32[]{:S(2)}, u32[]{:S(2)}) async-start(bf16[16,32,128]{2,1,0:T(8,128)(2,1)} %bitcast.4), calls=%async_computation.1 | async-start | bytes 262144 | tf_op jit(solution)/shard_map/all_to_all | solution.py:91
  69.8 63.0 %all-gather.8.cloned.1.call-start = ((), (), s32[]{:S(2)}) async-start(), calls=%async_computation.6 | async-start | bytes 1179648 | tf_op jit(solution)/shard_map/all_gather | solution.py:22
  80.6 14.7 %copy-start.2 = (bf16[32,2048]{1,0:T(8,128)(2,1)}, bf16[32,2048]{1,0:T(8,128)(2,1)S(1)}, u32[]{:S(2)}) copy-start(bf16[32,2048]{1,0:T(8,128)(2,1)S(1)} %get-tuple-element.6) | copy-start | bytes 393220
  80.6 14.6 %copy-start.11 = (f32[32]{0:T(128)}, f32[32]{0:T(128)S(1)}, u32[]{:S(2)}) copy-start(f32[32]{0:T(128)S(1)} %add_rsqrt_fusion.1) | copy-start | bytes 388
  96.1 58.6 %all-to-all-start.2 = ((bf16[32,12,2048]{2,1,0:T(8,128)(2,1)}), bf16[32,12,2048]{2,1,0:T(8,128)(2,1)S(1)}, u32[]{:S(2)}, u32[]{:S(2)}) async-start(bf16[32,12,2048]{2,1,0:T(8,128)(2,1)} %reshape.112), calls=%async_computation.2 | async-start | bytes 4194304 | tf_op jit(solution)/shard_map/all_to_all | solution.py:115
  105.8 76.3 %all-gather.10.cloned.1.call-start = ((), (), s32[]{:S(2)}) async-start(), calls=%async_computation.7 | async-start | bytes 1622016 | tf_op jit(solution)/shard_map/all_gather | solution.py:22
  132.8 8.9 %collective-permute-start.1 = (bf16[8,32,2048]{2,1,0:T(8,128)(2,1)}, bf16[8,32,2048]{2,1,0:T(8,128)(2,1)S(1)}, u32[]{:S(2)}, u32[]{:S(2)}) collective-permute-start(bf16[8,32,2048]{2,1,0:T(8,128)(2,1)} %bitcast.86), channel_id=1, source_target_pairs={{0,32},{32,0},{64,96},{96,64},{128,160},{160,128},{192,224},{224,1... | collective-permute-start | bytes 3145736 | tf_op jit(solution)/shard_map/ppermute | solution.py:15
  166.7 56.4 %all-to-all-start.3 = ((bf16[32,12,2048]{2,1,0:T(8,128)(2,1)}), bf16[32,12,2048]{2,1,0:T(8,128)(2,1)S(1)}, u32[]{:S(2)}, u32[]{:S(2)}) async-start(bf16[32,12,2048]{2,1,0:T(8,128)(2,1)} %reshape.114), calls=%async_computation.3 | async-start | bytes 4194304 | tf_op jit(solution)/shard_map/all_to_all | solution.py:124
  182.0 8.9 %copy-start.3 = (bf16[32,2048]{1,0:T(8,128)(2,1)S(1)}, bf16[32,2048]{1,0:T(8,128)(2,1)}, u32[]{:S(2)}) copy-start(bf16[32,2048]{1,0:T(8,128)(2,1)} %copy-done.2) | copy-start | bytes 393220
  182.0 8.9 %copy-start.12 = (f32[32]{0:T(128)S(1)}, f32[32]{0:T(128)}, u32[]{:S(2)}) copy-start(f32[32]{0:T(128)} %copy-done.11) | copy-start | bytes 388
  182.0 8.9 %copy-start.14 = (bf16[2048,32]{0,1:T(8,128)(2,1)S(1)}, bf16[2048,32]{0,1:T(8,128)(2,1)}, u32[]{:S(2)}) copy-start(bf16[2048,32]{0,1:T(8,128)(2,1)} %param.16) | copy-start | bytes 393220
  182.0 9.4 %copy-start.1 = (bf16[4096,176]{0,1:T(8,128)(2,1)S(1)}, bf16[4096,176]{0,1:T(8,128)(2,1)}, u32[]{:S(2)}) copy-start(bf16[4096,176]{0,1:T(8,128)(2,1)} %all-gather.10.cloned.1.call-done) | copy-start | bytes 4325380
  183.6 9.9 %collective-permute-start.2 = (bf16[8,512,176]{1,2,0:T(8,128)(2,1)S(1)}, bf16[8,512,176]{1,2,0:T(8,128)(2,1)S(1)}, u32[]{:S(2)}, u32[]{:S(2)}) collective-permute-start(bf16[8,512,176]{1,2,0:T(8,128)(2,1)S(1)} %bitcast.83), channel_id=1, source_target_pairs={{0,32},{32,0},{64,96},{96,64},{128,160},{160,128},{192,224},{224,1... | collective-permute-start | bytes 4325384 | tf_op jit(solution)/shard_map/ppermute | solution.py:15
  193.9 1.1 copy-start.4
  223.1 16.0 %all-to-all-start.4 = ((bf16[16,32,128]{2,1,0:T(8,128)(2,1)}), bf16[16,32,128]{2,1,0:T(8,128)(2,1)}, u32[]{:S(2)}, u32[]{:S(2)}) async-start(bf16[16,32,128]{2,1,0:T(8,128)(2,1)} %bitcast.90), calls=%async_computation.4 | async-start | bytes 262144 | tf_op jit(solution)/shard_map/all_to_all | solution.py:141
  230.5 10.9 %copy-start.9 = (f32[2048]{0:T(1024)S(1)}, f32[2048]{0:T(1024)}, u32[]{:S(2)}) copy-start(f32[2048]{0:T(1024)} %param.23) | copy-start | bytes 24580
Sparse Core Ops, SparseCore 0:
  9.7 83.6 all-gather.5
  96.2 36.5 all-gather.7
  145.5 36.4 all-gather.9
where the time goes:
time: 250 us; the launch traced here: 249 us
  waiting for transfers between devices  101 us (40%)
  starting transfers between devices  46.9 us (19%)
  blocking collectives  44.2 us (18%)
  matrix products  16.3 us (7%)
  between operations  15.4 us (6%)
  local copies, waits for them, and re-layouts  14.8 us (6%)
  other arithmetic  9.99 us (4%)
    all_to_all x1, blocking collectives, pair_collect(): lax.all_to_all(copies, axis, 0, 0, tiled=True, axis_index_groups=core_gro...  44.2 us
    all_gather x2, waiting for transfers between devices, pair_gather(): lax.all_gather(array, axis, axis=0, axis_index_groups=core_groups(axis))  34.7 us
    all_to_all x1, waiting for transfers between devices, per_device(): lax.all_to_all(result, 'expert', split_axis=0, concat_axis=0, tiled=True)  26.5 us
    ppermute x3, starting transfers between devices, with_sibling(): lax.ppermute(blocks, axis, [(i, i ^ 1) for i in range(lax.axis_size(axis))])  19.2 us
    all_to_all x1, starting transfers between devices, per_device(): lax.all_to_all(outgoing, 'expert', split_axis=0, concat_axis=0, tiled=True)  9.68 us
    all_to_all x1, waiting for transfers between devices, per_device(): lax.all_to_all(outgoing, 'expert', split_axis=0, concat_axis=0, tiled=True)  9.27 us
    all_to_all x1, waiting for transfers between devices, per_device(): lax.all_to_all(proj_cols, 'dp', split_axis=0, concat_axis=1, tiled=True)  8.85 us
    all_gather x1, waiting for transfers between devices, per_device(): weights_full = lax.all_gather(weights_part, 'dp', axis=0, tiled=True)  8.74 us
  transfers between devices with their start and end apart: 10, of which 10 were waited for; matrix products, arithmetic and copies ran while one was open for 13% of the time, Pallas kernels for 0%

commit v1 on v0

--- a/solution.py
+++ b/solution.py
@@ -109,7 +109,9 @@
     outgoing = outgoing.astype(jnp.bfloat16).reshape(experts, capacity, width)
     hidden_units = expert_down.shape[1]
     weights_part = jnp.concatenate([expert_gate_up[0], expert_down[0].T], axis=1)
-    weights_full = lax.all_gather(weights_part, "dp", axis=0, tiled=True)
+    weights_full = jnp.concatenate(
+        lax.all_to_all(jnp.stack([weights_part] * lax.axis_size("dp")), "dp", 0, 0), axis=0
+    )
     gate_up_full = weights_full[:, : 2 * hidden_units]
     down_turned_full = weights_full[:, 2 * hidden_units :]
     received = lax.all_to_all(outgoing, "expert", split_axis=0, concat_axis=0, tiled=True)

time: 250 us -> 435 us (1.74)
  waiting for transfers between devices: 101 us -> 271 us
  local copies, waits for them, and re-layouts: 14.8 us -> 33.5 us
  blocking collectives: 44.2 us -> 37.9 us
    all_to_all x0 -> x1, waiting for transfers between devices: none -> 181 us  [per_device(): lax.all_to_all(jnp.stack([weights_part] * lax.axis_size('dp')), 'dp', 0, 0)]
    all_to_all x0 -> x1, local copies, waits for them, and re-layouts: none -> 11.7 us  [per_device(): lax.all_to_all(jnp.stack([weights_part] * lax.axis_size('dp')), 'dp', 0, 0)]
    all_gather x1 -> x0, waiting for transfers between devices: 8.74 us -> none  [per_device(): weights_full = lax.all_gather(weights_part, 'dp', axis=0, tiled=True)]
    all_to_all x1, blocking collectives: 44.2 us -> 37.9 us  [pair_collect(): lax.all_to_all(copies, axis, 0, 0, tiled=True, axis_index_groups=core_gro...]
    another operation x1 -> x2, local copies, waits for them, and re-layouts: 0.01 us -> 5 us  [the longest x1 4.99 us: per_device(): jnp.stack([weights_part] * lax.axis_size('dp'))]
    all_to_all x0 -> x1, starting transfers between devices: none -> 4.79 us  [per_device(): lax.all_to_all(jnp.stack([weights_part] * lax.axis_size('dp')), 'dp', 0, 0)]
  transfers between devices with their start and end apart: 10 -> 10, of which waited for: 10 -> 10; matrix products, arithmetic and copies ran while one was open for 13% -> 7% of each run, Pallas kernels for 0% -> 0%
where the time goes in v1:
time: 435 us; the launch traced here: 434 us
  waiting for transfers between devices  271 us (62%)
  starting transfers between devices  51.2 us (12%)
  blocking collectives  37.9 us (9%)
  local copies, waits for them, and re-layouts  33.5 us (8%)
  matrix products  16.3 us (4%)
  between operations  15.8 us (4%)
  other arithmetic  8.19 us (2%)
    all_to_all x1, waiting for transfers between devices, per_device(): lax.all_to_all(jnp.stack([weights_part] * lax.axis_size('dp')), 'dp', 0, 0)  181 us
    all_to_all x1, blocking collectives, pair_collect(): lax.all_to_all(copies, axis, 0, 0, tiled=True, axis_index_groups=core_gro...  37.9 us
    all_gather x2, waiting for transfers between devices, pair_gather(): lax.all_gather(array, axis, axis=0, axis_index_groups=core_groups(axis))  36.8 us
    all_to_all x1, waiting for transfers between devices, per_device(): lax.all_to_all(result, 'expert', split_axis=0, concat_axis=0, tiled=True)  24.9 us
    ppermute x3, starting transfers between devices, with_sibling(): lax.ppermute(blocks, axis, [(i, i ^ 1) for i in range(lax.axis_size(axis))])  18.4 us
    all_to_all x1, local copies, waits for them, and re-layouts, per_device(): lax.all_to_all(jnp.stack([weights_part] * lax.axis_size('dp')), 'dp', 0, 0)  11.7 us
    all_to_all x1, starting transfers between devices, per_device(): lax.all_to_all(outgoing, 'expert', split_axis=0, concat_axis=0, tiled=True)  9.68 us
    all_to_all x1, waiting for transfers between devices, per_device(): lax.all_to_all(proj_cols, 'dp', split_axis=0, concat_axis=1, tiled=True)  8.86 us
  transfers between devices with their start and end apart: 10, of which 10 were waited for; matrix products, arithmetic and copies ran while one was open for 7% of the time, Pallas kernels for 0%

profile of v1, /device:TPU:1, one launch (start us, length us, event | category | flops | bytes accessed | tf_op | source)
XLA Modules:
  0.0 433.5 jit_solution(6776661390882591521)
XLA Ops:
  7.7 37.9 %all_to_all.46 = bf16[8,32,2048]{2,1,0:T(8,128)(2,1)S(1)} all-to-all(bf16[8,32,2048]{2,1,0:T(8,128)(2,1)S(1)} %broadcast_in_dim.26), channel_id=1, replica_groups={{0,64,128,192,256,320,384,448},{32,96,160,224,288,352,416,480},{1,65,12..., dimensions={0} | all-to-all | bytes 2097152 | tf_op jit(solution)/shard_map/all_to_all | solution.py:28
  45.6 4.4 %collective-permute-start = (bf16[8,32,2048]{2,1,0:T(8,128)(2,1)S(1)}, bf16[8,32,2048]{2,1,0:T(8,128)(2,1)S(1)}, u32[]{:S(2)}, u32[]{:S(2)}) collective-permute-start(bf16[8,32,2048]{2,1,0:T(8,128)(2,1)S(1)} %all_to_all.46), channel_id=1, source_target_pairs={{0,32},{32,0},{64,96},{96,64},{128,160},{160,128},{192,224},{224,1... | collective-permute-start | bytes 3145736 | tf_op jit(solution)/shard_map/ppermute | solution.py:15
  49.9 1.7 copy.45
  53.4 1.4 convolution_convert_fusion.1
  54.8 3.7 all-to-all-start.1
  58.8 8.9 %all-to-all-done.1 = bf16[16,32,128]{2,1,0:T(8,128)(2,1)S(1)} async-done(((bf16[16,32,128]{2,1,0:T(8,128)(2,1)}), bf16[16,32,128]{2,1,0:T(8,128)(2,1)S(1)}, u32[]{:S(2)}, u32[]{:S(2)}) %all-to-all-start.1) | async-done | bytes 131104 | tf_op jit(solution)/shard_map/all_to_all | solution.py:91
  67.7 5.0 %stack.23 = bf16[16,128,2112]{1,2,0:T(8,128)(2,1)} broadcast(bf16[128,2112]{0,1:T(8,128)(2,1)S(1)} %copy.46), dimensions={1,2} | broadcast | bytes 9191424 | tf_op jit(solution)/shard_map/stack | solution.py:113
  72.7 4.8 %all-to-all-start.3 = ((bf16[16,128,2112]{1,2,0:T(8,128)(2,1)}), bf16[16,128,2112]{1,2,0:T(8,128)(2,1)}, u32[]{:S(2)}, u32[]{:S(2)}) async-start(bf16[16,128,2112]{1,2,0:T(8,128)(2,1)} %stack.23), calls=%async_computation.3 | async-start | bytes 17301504 | tf_op jit(solution)/shard_map/all_to_all | solution.py:113
  82.1 1.5 reshape.117
  83.6 1.3 slice.56
  85.6 180.6 %all-to-all-done.3 = bf16[16,128,2112]{1,2,0:T(8,128)(2,1)} async-done(((bf16[16,128,2112]{1,2,0:T(8,128)(2,1)}), bf16[16,128,2112]{1,2,0:T(8,128)(2,1)}, u32[]{:S(2)}, u32[]{:S(2)}) %all-to-all-start.3) | async-done | bytes 8650784 | tf_op jit(solution)/shard_map/all_to_all | solution.py:113
  266.2 11.7 %copy.47 = bf16[16,128,2112]{2,1,0:T(8,128)(2,1)} copy(bf16[16,128,2112]{1,2,0:T(8,128)(2,1)} %all-to-all-done.3) | data formatting | bytes 17301504 | tf_op jit(solution)/shard_map/all_to_all | solution.py:113
  280.5 9.7 %all-to-all-start.2 = ((bf16[32,12,2048]{2,1,0:T(8,128)(2,1)}), bf16[32,12,2048]{2,1,0:T(8,128)(2,1)S(1)}, u32[]{:S(2)}, u32[]{:S(2)}) async-start(bf16[32,12,2048]{2,1,0:T(8,128)(2,1)} %reshape.117), calls=%async_computation.2 | async-start | bytes 4194304 | tf_op jit(solution)/shard_map/all_to_all | solution.py:117
  290.3 27.6 %all-gather.5.cloned.1.call-done = bf16[256,2048]{1,0:T(8,128)(2,1)} async-done(((bf16[32,2048]{1,0:T(8,128)(2,1)}), bf16[256,2048]{1,0:T(8,128)(2,1)}) %all-gather.5.cloned.1.call-update) | async-done | bytes 1048592 | tf_op jit(solution)/shard_map/all_gather | solution.py:22
  317.9 6.7 %collective-permute-start.1 = (bf16[8,32,2048]{2,1,0:T(8,128)(2,1)}, bf16[8,32,2048]{2,1,0:T(8,128)(2,1)S(1)}, u32[]{:S(2)}, u32[]{:S(2)}) collective-permute-start(bf16[8,32,2048]{2,1,0:T(8,128)(2,1)} %bitcast.90), channel_id=1, source_target_pairs={{0,32},{32,0},{64,96},{96,64},{128,160},{160,128},{192,224},{224,1... | collective-permute-start | bytes 3145736 | tf_op jit(solution)/shard_map/ppermute | solution.py:15
  324.6 2.5 collective-permute-done.1
  327.1 1.4 pad_maximum_fusion.2
  330.9 8.1 %all-to-all-done.2 = bf16[32,12,2048]{2,1,0:T(8,128)(2,1)S(1)} async-done(((bf16[32,12,2048]{2,1,0:T(8,128)(2,1)}), bf16[32,12,2048]{2,1,0:T(8,128)(2,1)S(1)}, u32[]{:S(2)}, u32[]{:S(2)}) %all-to-all-start.2) | async-done | bytes 1572896 | tf_op jit(solution)/shard_map/all_to_all | solution.py:117
  338.9 1.4 reshape.118
  340.3 5.8 %fusion = f32[384,1408]{1,0:T(8,128)S(1)} fusion(bf16[384,2048]{1,0:T(8,128)(2,1)} %reshape.118, bf16[2048,2112]{1,0:T(8,128)(2,1)} %bitcast.79), kind=kOutput, calls=%fused_computation | convolution fusion | flops 2214592512 | bytes 9502720 | tf_op jit(solution)/shard_map/dot_general | solution.py:120
  346.1 3.3 fusion.4
  349.4 1.5 reshape.120
  350.9 7.0 %all-to-all-start.4 = ((bf16[32,12,2048]{2,1,0:T(8,128)(2,1)}), bf16[32,12,2048]{2,1,0:T(8,128)(2,1)S(1)}, u32[]{:S(2)}, u32[]{:S(2)}) async-start(bf16[32,12,2048]{2,1,0:T(8,128)(2,1)} %reshape.120), calls=%async_computation.4 | async-start | bytes 4194304 | tf_op jit(solution)/shard_map/all_to_all | solution.py:126
  358.0 9.1 %all-gather.7.cloned.1.call-done = bf16[4096,176]{0,1:T(8,128)(2,1)} async-done(((bf16[512,176]{0,1:T(8,128)(2,1)}), bf16[4096,176]{0,1:T(8,128)(2,1)}) %all-gather.7.cloned.1.call-update) | async-done | bytes 1441808 | tf_op jit(solution)/shard_map/all_gather | solution.py:22
  367.1 1.6 copy.64
  368.8 7.3 %collective-permute-start.2 = (bf16[8,512,176]{1,2,0:T(8,128)(2,1)S(1)}, bf16[8,512,176]{1,2,0:T(8,128)(2,1)S(1)}, u32[]{:S(2)}, u32[]{:S(2)}) collective-permute-start(bf16[8,512,176]{1,2,0:T(8,128)(2,1)S(1)} %bitcast.87), channel_id=1, source_target_pairs={{0,32},{32,0},{64,96},{96,64},{128,160},{160,128},{192,224},{224,1... | collective-permute-start | bytes 4325384 | tf_op jit(solution)/shard_map/ppermute | solution.py:15
  380.1 1.6 convolution_convert_fusion.2
  381.7 24.9 %all-to-all-done.4 = bf16[32,12,2048]{2,1,0:T(8,128)(2,1)S(1)} async-done(((bf16[32,12,2048]{2,1,0:T(8,128)(2,1)}), bf16[32,12,2048]{2,1,0:T(8,128)(2,1)S(1)}, u32[]{:S(2)}, u32[]{:S(2)}) %all-to-all-start.4) | async-done | bytes 1572896 | tf_op jit(solution)/shard_map/all_to_all | solution.py:126
  406.6 7.6 %all-to-all-start.5 = ((bf16[16,32,128]{2,1,0:T(8,128)(2,1)}), bf16[16,32,128]{2,1,0:T(8,128)(2,1)}, u32[]{:S(2)}, u32[]{:S(2)}) async-start(bf16[16,32,128]{2,1,0:T(8,128)(2,1)} %bitcast.24), calls=%async_computation.5 | async-start | bytes 262144 | tf_op jit(solution)/shard_map/all_to_all | solution.py:143
  415.0 1.3 reshape.121
  416.3 7.2 %all-to-all-done.5 = bf16[16,32,128]{2,1,0:T(8,128)(2,1)} async-done(((bf16[16,32,128]{2,1,0:T(8,128)(2,1)}), bf16[16,32,128]{2,1,0:T(8,128)(2,1)}, u32[]{:S(2)}, u32[]{:S(2)}) %all-to-all-start.5) | async-done | bytes 131104 | tf_op jit(solution)/shard_map/all_to_all | solution.py:143
  423.5 2.4 multiply_reduce_fusion
  (81 shorter events, 16.8 us)
Async XLA Ops:
  6.5 322.6 %copy-start = (bf16[2048,2,176]{0,2,1:T(8,128)(2,1)S(1)}, bf16[2048,2,176]{0,2,1:T(8,128)(2,1)}, u32[]{:S(2)}) copy-start(bf16[2048,2,176]{0,2,1:T(8,128)(2,1)} %param.21) | copy-start | bytes 4325380
  45.6 6.6 %collective-permute-start = (bf16[8,32,2048]{2,1,0:T(8,128)(2,1)S(1)}, bf16[8,32,2048]{2,1,0:T(8,128)(2,1)S(1)}, u32[]{:S(2)}, u32[]{:S(2)}) collective-permute-start(bf16[8,32,2048]{2,1,0:T(8,128)(2,1)S(1)} %all_to_all.46), channel_id=1, source_target_pairs={{0,32},{32,0},{64,96},{96,64},{128,160},{160,128},{192,224},{224,1... | collective-permute-start | bytes 3145736 | tf_op jit(solution)/shard_map/ppermute | solution.py:15
  52.4 1.0 copy-start.7
  53.0 5.5 %copy-start.5 = (bf16[128,704]{1,0:T(8,128)(2,1)S(1)}, bf16[128,704]{1,0:T(8,128)(2,1)}, u32[]{:S(2)}) copy-start(bf16[128,704]{1,0:T(8,128)(2,1)} %copy.45) | copy-start | bytes 540676
  53.0 5.5 %copy-start.8 = (bf16[1,128,1408]{2,1,0:T(8,128)(2,1)S(1)}, bf16[1,128,1408]{2,1,0:T(8,128)(2,1)}, u32[]{:S(2)}) copy-start(bf16[1,128,1408]{2,1,0:T(8,128)(2,1)} %param.19) | copy-start | bytes 1081348
  54.8 12.9 %all-to-all-start.1 = ((bf16[16,32,128]{2,1,0:T(8,128)(2,1)}), bf16[16,32,128]{2,1,0:T(8,128)(2,1)S(1)}, u32[]{:S(2)}, u32[]{:S(2)}) async-start(bf16[16,32,128]{2,1,0:T(8,128)(2,1)} %bitcast.4), calls=%async_computation.1 | async-start | bytes 262144 | tf_op jit(solution)/shard_map/all_to_all | solution.py:91
  72.7 6.8 %copy-start.12 = (s32[32,6]{0,1:T(8,128)S(1)}, s32[32,6]{0,1:T(8,128)}, u32[]{:S(2)}) copy-start(s32[32,6]{0,1:T(8,128)} %param.17) | copy-start | bytes 2308
  72.7 6.8 %copy-start.15 = (s32[32]{0:T(128)S(1)}, s32[32]{0:T(128)}, u32[]{:S(2)}) copy-start(s32[32]{0:T(128)} %param.18) | copy-start | bytes 388
  72.7 8.6 %copy-start.9 = (bf16[32,2048]{1,0:T(8,128)(2,1)S(1)}, bf16[32,2048]{1,0:T(8,128)(2,1)}, u32[]{:S(2)}) copy-start(bf16[32,2048]{1,0:T(8,128)(2,1)} %param.12) | copy-start | bytes 393220
  72.7 8.8 %copy-start.10 = (f32[2048]{0:T(1024)S(1)}, f32[2048]{0:T(1024)}, u32[]{:S(2)}) copy-start(f32[2048]{0:T(1024)} %param.15) | copy-start | bytes 24580
  72.7 193.6 %all-to-all-start.3 = ((bf16[16,128,2112]{1,2,0:T(8,128)(2,1)}), bf16[16,128,2112]{1,2,0:T(8,128)(2,1)}, u32[]{:S(2)}, u32[]{:S(2)}) async-start(bf16[16,128,2112]{1,2,0:T(8,128)(2,1)} %stack.23), calls=%async_computation.3 | async-start | bytes 17301504 | tf_op jit(solution)/shard_map/all_to_all | solution.py:113
  77.5 240.4 %all-gather.5.cloned.1.call-start = ((), (), s32[]{:S(2)}) async-start(), calls=%async_computation.6 | async-start | bytes 1179648 | tf_op jit(solution)/shard_map/all_gather | solution.py:22
  81.4 198.3 %copy-start.3 = (bf16[32,2048]{1,0:T(8,128)(2,1)}, bf16[32,2048]{1,0:T(8,128)(2,1)S(1)}, u32[]{:S(2)}) copy-start(bf16[32,2048]{1,0:T(8,128)(2,1)S(1)} %get-tuple-element.6) | copy-start | bytes 393220
  81.5 198.3 %copy-start.13 = (f32[32]{0:T(128)}, f32[32]{0:T(128)S(1)}, u32[]{:S(2)}) copy-start(f32[32]{0:T(128)S(1)} %add_rsqrt_fusion.1) | copy-start | bytes 388
  280.5 58.4 %all-to-all-start.2 = ((bf16[32,12,2048]{2,1,0:T(8,128)(2,1)}), bf16[32,12,2048]{2,1,0:T(8,128)(2,1)S(1)}, u32[]{:S(2)}, u32[]{:S(2)}) async-start(bf16[32,12,2048]{2,1,0:T(8,128)(2,1)} %reshape.117), calls=%async_computation.2 | async-start | bytes 4194304 | tf_op jit(solution)/shard_map/all_to_all | solution.py:117
  290.2 76.9 %all-gather.7.cloned.1.call-start = ((), (), s32[]{:S(2)}) async-start(), calls=%async_computation.7 | async-start | bytes 1622016 | tf_op jit(solution)/shard_map/all_gather | solution.py:22
  317.9 9.2 %collective-permute-start.1 = (bf16[8,32,2048]{2,1,0:T(8,128)(2,1)}, bf16[8,32,2048]{2,1,0:T(8,128)(2,1)S(1)}, u32[]{:S(2)}, u32[]{:S(2)}) collective-permute-start(bf16[8,32,2048]{2,1,0:T(8,128)(2,1)} %bitcast.90), channel_id=1, source_target_pairs={{0,32},{32,0},{64,96},{96,64},{128,160},{160,128},{192,224},{224,1... | collective-permute-start | bytes 3145736 | tf_op jit(solution)/shard_map/ppermute | solution.py:15
  350.9 55.7 %all-to-all-start.4 = ((bf16[32,12,2048]{2,1,0:T(8,128)(2,1)}), bf16[32,12,2048]{2,1,0:T(8,128)(2,1)S(1)}, u32[]{:S(2)}, u32[]{:S(2)}) async-start(bf16[32,12,2048]{2,1,0:T(8,128)(2,1)} %reshape.120), calls=%async_computation.4 | async-start | bytes 4194304 | tf_op jit(solution)/shard_map/all_to_all | solution.py:126
  367.1 8.9 %copy-start.4 = (bf16[32,2048]{1,0:T(8,128)(2,1)S(1)}, bf16[32,2048]{1,0:T(8,128)(2,1)}, u32[]{:S(2)}) copy-start(bf16[32,2048]{1,0:T(8,128)(2,1)} %copy-done.3) | copy-start | bytes 393220
  367.1 8.9 %copy-start.14 = (f32[32]{0:T(128)S(1)}, f32[32]{0:T(128)}, u32[]{:S(2)}) copy-start(f32[32]{0:T(128)} %copy-done.13) | copy-start | bytes 388
  367.1 8.9 %copy-start.16 = (bf16[2048,32]{0,1:T(8,128)(2,1)S(1)}, bf16[2048,32]{0,1:T(8,128)(2,1)}, u32[]{:S(2)}) copy-start(bf16[2048,32]{0,1:T(8,128)(2,1)} %param.16) | copy-start | bytes 393220
  367.1 9.4 %copy-start.2 = (bf16[4096,176]{0,1:T(8,128)(2,1)S(1)}, bf16[4096,176]{0,1:T(8,128)(2,1)}, u32[]{:S(2)}) copy-start(bf16[4096,176]{0,1:T(8,128)(2,1)} %all-gather.7.cloned.1.call-done) | copy-start | bytes 4325380
  368.8 9.9 %collective-permute-start.2 = (bf16[8,512,176]{1,2,0:T(8,128)(2,1)S(1)}, bf16[8,512,176]{1,2,0:T(8,128)(2,1)S(1)}, u32[]{:S(2)}, u32[]{:S(2)}) collective-permute-start(bf16[8,512,176]{1,2,0:T(8,128)(2,1)S(1)} %bitcast.87), channel_id=1, source_target_pairs={{0,32},{32,0},{64,96},{96,64},{128,160},{160,128},{192,224},{224,1... | collective-permute-start | bytes 4325384 | tf_op jit(solution)/shard_map/ppermute | solution.py:15
  379.0 1.1 copy-start.6
  406.6 16.9 %all-to-all-start.5 = ((bf16[16,32,128]{2,1,0:T(8,128)(2,1)}), bf16[16,32,128]{2,1,0:T(8,128)(2,1)}, u32[]{:S(2)}, u32[]{:S(2)}) async-start(bf16[16,32,128]{2,1,0:T(8,128)(2,1)} %bitcast.24), calls=%async_computation.5 | async-start | bytes 262144 | tf_op jit(solution)/shard_map/all_to_all | solution.py:143
  415.0 10.9 %copy-start.11 = (f32[2048]{0:T(1024)S(1)}, f32[2048]{0:T(1024)}, u32[]{:S(2)}) copy-start(f32[2048]{0:T(1024)} %param.23) | copy-start | bytes 24580
  415.0 11.7 %copy-start.1 = (bf16[2048,2,176]{0,2,1:T(8,128)(2,1)S(1)}, bf16[2048,2,176]{0,2,1:T(8,128)(2,1)}, u32[]{:S(2)}) copy-start(bf16[2048,2,176]{0,2,1:T(8,128)(2,1)} %param.21) | copy-start | bytes 4325380
Sparse Core Ops, SparseCore 0:
  280.6 37.1 all-gather.4
  331.0 36.0 all-gather.6
